TPU v7x, 512 devices: a whole 4x8x8 slice. The times are simulated.
512 devices in a mesh: seq: 128 (over z, y, core), tp: 4 (over x).
Axes of the slice: x: 4, y: 8, z: 8, core: 2. Of those that a mesh axis runs over, the one named last changes fastest.
Arguments:
- hidden_in: bfloat16 [16384, 1536], P('seq'), may hold values from -6 to 6
- w_query: bfloat16 [1536, 1536], P(None, 'tp'), may hold values from -0.625 to 0.625
- key_weight: bfloat16 [1536, 512], P(None, 'tp'), may hold values from -0.625 to 0.625
- value_weight: bfloat16 [1536, 512], P(None, 'tp'), may hold values from -0.15625 to 0.15625
- w_out: bfloat16 [1536, 1536], P('tp'), may hold values from -0.4375 to 0.4375
- cached_prefix_keys: bfloat16 [4096, 512], P('seq', 'tp'), may hold values from -60000 to 60000
- cached_prefix_values: bfloat16 [4096, 512], P('seq', 'tp'), may hold values from -6 to 6
- doc_ids: int32 [128, 128], P('seq'), may hold values from 0 to 3, never falling along the last dimension, each value on 1 to 64 neighbouring positions
- routes: int32 [16384, 8], P(('seq', 'tp')), may hold values from 0 to 31, all different within a row; in each aligned block of 32 rows (0 to 31, 32 to 63, ...) at most 16 rows name the same one
- gate_scores: float32 [16384, 8], P(('seq', 'tp')), may hold values from 0.2 to 1
- expert_in: bfloat16 [128, 1536, 256], P('seq'), may hold values from -0.15625 to 0.15625
- expert_out: bfloat16 [128, 128, 1536], P('seq'), may hold values from -0.25 to 0.25
Outputs:
- attn_proj: bfloat16 [16384, 1536], P(('seq', 'tp'))
- expert_mix: bfloat16 [16384, 1536], P(('seq', 'tp'))
- layer_out: bfloat16 [16384, 1536], P(('seq', 'tp'))
Inputs may be any that keep to these rules, and one draw needn't show every extreme that they name: `routes`: within the rows of one device (aligned blocks of 32 tokens) no expert is picked by more than 16 tokens, a bound that some block reaches; every expert is picked somewhere.
All inputs are finite; a program needn't handle non-finite values.
Results may differ from a plain program's by a relative error of at most 0.028.
Values may be sent and summed in bfloat16 or wider, within the bound.
No kernel may reach another device: no remote copies, remote signals or barrier semaphores. Data moves between devices by JAX's collectives and lax.ppermute only.
A program may use at most 64 MiB of HBM per device.

v0:
```python
import jax
import jax.numpy as jnp
from jax import lax
from jax.sharding import Mesh, PartitionSpec as P

HEAD_WIDTH = 64
EXPERTS = 32
SEQ = ("z", "yh", "yl", "c")
EXPERT_AXES = ("z", "yh")
PART_AXES = ("yl", "c")
EPSILON = 1e-06
RESIDUAL = 0.22


def normalize(values):
    values = values.astype(jnp.float32)
    return values * lax.rsqrt(jnp.mean(values * values, axis=-1, keepdims=True) + EPSILON)


def rotary_apply(values, token_positions):
    half_size = values.shape[-1] // 2
    frequency = jnp.exp(
        -jnp.log(10000.0) * jnp.arange(half_size, dtype=jnp.float32) * 2.0 / values.shape[-1]
    )
    angles = token_positions[:, None] * frequency[None, :]
    cosine = jnp.cos(angles)[:, None, :]
    sine_part = jnp.sin(angles)[:, None, :]
    first_half = values[..., :half_size]
    second = values[..., half_size:]
    return jnp.concatenate(
        [first_half * cosine - second * sine_part, second * cosine + first_half * sine_part],
        axis=-1,
    )


def body(
    hidden_in,
    w_query,
    key_weight,
    value_weight,
    w_out,
    cached_prefix_keys,
    cached_prefix_values,
    doc_ids,
    routes,
    gate_scores,
    expert_in,
    expert_out,
):
    rows_dev = hidden_in.shape[0]
    column_list = hidden_in.shape[1]
    head_size = HEAD_WIDTH
    kv_local = key_weight.shape[1] // head_size
    group_width = w_query.shape[1] // head_size // kv_local
    seq_count = lax.axis_size(SEQ)
    prefix_len = cached_prefix_keys.shape[0] * seq_count
    doc_row = doc_ids[0]
    row_index = jnp.arange(rows_dev, dtype=jnp.int32)
    same_doc = doc_row[:, None] == doc_row[None, :]
    doc_start = jnp.min(jnp.where(same_doc, row_index[None, :], rows_dev), axis=1)
    token_positions = (prefix_len + row_index - doc_start).astype(jnp.float32)
    normed_input = normalize(hidden_in).astype(jnp.bfloat16)
    query_rows_all = jnp.dot(normed_input, w_query, preferred_element_type=jnp.float32).reshape(
        rows_dev, kv_local * group_width, head_size
    )
    query_rows_all = (
        rotary_apply(query_rows_all, token_positions)
        .astype(jnp.bfloat16)
        .reshape(rows_dev, kv_local, group_width, head_size)
    )
    fresh_key = jnp.dot(normed_input, key_weight, preferred_element_type=jnp.float32).reshape(
        rows_dev, kv_local, head_size
    )
    fresh_key = rotary_apply(fresh_key, token_positions).astype(jnp.bfloat16)
    fresh_value = (
        jnp.dot(normed_input, value_weight, preferred_element_type=jnp.float32)
        .astype(jnp.bfloat16)
        .reshape(rows_dev, kv_local, head_size)
    )
    own_scores = (
        jnp.einsum("tkgd,skd->tkgs", query_rows_all, fresh_key, preferred_element_type=jnp.float32)
        / head_size
    )
    visible = same_doc & (row_index[None, :] <= row_index[:, None])
    own_scores = jnp.where(visible[:, None, None, :], own_scores, -jnp.inf)
    row_top = jnp.max(own_scores, axis=-1)
    weights = jnp.exp(own_scores - row_top[..., None])
    denominator = jnp.sum(weights, axis=-1)
    numerator = jnp.einsum(
        "tkgs,skd->tkgd",
        weights.astype(jnp.bfloat16),
        fresh_value,
        preferred_element_type=jnp.float32,
    )
    running = (row_top, denominator, numerator)
    prefix_both = jnp.concatenate([cached_prefix_keys, cached_prefix_values], axis=1)
    whole_both = lax.all_gather(prefix_both, SEQ, axis=0, tiled=True)
    kv_cols = cached_prefix_keys.shape[1]
    whole_keys = whole_both[:, :kv_cols]
    whole_values = whole_both[:, kv_cols:]
    top_old, denom_old, numer_old = running
    key_rows = whole_keys.reshape(-1, kv_local, head_size)
    value_rows = whole_values.reshape(-1, kv_local, head_size)
    scores = (
        jnp.einsum("tkgd,pkd->tkgp", query_rows_all, key_rows, preferred_element_type=jnp.float32)
        / head_size
    )
    top_new = jnp.maximum(top_old, jnp.max(scores, axis=-1))
    shrink = jnp.exp(top_old - top_new)
    part_weights = jnp.exp(scores - top_new[..., None])
    denom_new = denom_old * shrink + jnp.sum(part_weights, axis=-1)
    numer_new = numer_old * shrink[..., None] + jnp.einsum(
        "tkgp,pkd->tkgd",
        part_weights.astype(jnp.bfloat16),
        value_rows,
        preferred_element_type=jnp.float32,
    )
    running = (top_new, denom_new, numer_new)
    attended = (
        (running[2] / running[1][..., None])
        .astype(jnp.bfloat16)
        .reshape(rows_dev, kv_local * group_width * head_size)
    )
    moe_rows = routes.shape[0]
    row_start = lax.axis_index("tp") * moe_rows
    attn_sum = lax.psum_scatter(
        jnp.dot(attended, w_out, preferred_element_type=jnp.float32),
        "tp",
        scatter_dimension=0,
        tiled=True,
    )
    residual = (
        lax.dynamic_slice_in_dim(hidden_in, row_start, moe_rows, 0).astype(jnp.float32)
        + RESIDUAL * attn_sum
    )
    routed = normalize(residual).astype(jnp.bfloat16)
    experts = EXPERTS
    capacity = moe_rows // 2
    ff_part = expert_out.shape[1]
    onehot = (routes[:, :, None] == jnp.arange(experts, dtype=jnp.int32)[None, None, :]).astype(
        jnp.int32
    )
    per_row = jnp.sum(onehot, axis=1)
    before = jnp.cumsum(per_row, axis=0) - per_row
    rank_in = jnp.sum(onehot * before[:, None, :], axis=2)
    slot_of = routes * capacity + rank_in
    slot_ids = jnp.arange(experts * capacity, dtype=jnp.int32)
    pick_hit = slot_of[:, :, None] == slot_ids[None, None, :]
    selector = jnp.any(pick_hit, axis=1).T.astype(jnp.bfloat16)
    combiner = jnp.sum(jnp.where(pick_hit, gate_scores[:, :, None], 0.0), axis=1)
    gathered = jnp.dot(selector, routed, preferred_element_type=jnp.float32).astype(jnp.bfloat16)
    outgoing = gathered.reshape(experts, capacity, column_list)
    incoming = lax.all_to_all(outgoing, EXPERT_AXES, split_axis=0, concat_axis=0, tiled=True)
    incoming = incoming.reshape(experts * capacity, column_list)
    full_in = lax.all_gather(expert_in, PART_AXES, axis=0, tiled=True)
    full_out = lax.all_gather(expert_out, PART_AXES, axis=0, tiled=True)
    gate_up = jnp.einsum("rd,pdf->prf", incoming, full_in, preferred_element_type=jnp.float32)
    activated = (jax.nn.silu(gate_up[..., :ff_part]) * gate_up[..., ff_part:]).astype(jnp.bfloat16)
    partial_value = jnp.einsum(
        "prf,pfd->prd", activated, full_out, preferred_element_type=jnp.float32
    ).astype(jnp.bfloat16)
    part_total = jnp.sum(partial_value.astype(jnp.float32), axis=0).astype(jnp.bfloat16)
    returned = lax.all_to_all(
        part_total.reshape(experts, capacity, column_list),
        EXPERT_AXES,
        split_axis=0,
        concat_axis=0,
        tiled=True,
    )
    part_sum = returned.reshape(experts * capacity, column_list).astype(jnp.float32)
    expert_sum = jnp.dot(
        combiner, part_sum, precision=lax.Precision.HIGHEST, preferred_element_type=jnp.float32
    )
    layer_out = (residual + RESIDUAL * expert_sum).astype(jnp.bfloat16)
    return (attn_sum.astype(jnp.bfloat16), expert_sum.astype(jnp.bfloat16), layer_out)


def solution(mesh):
    seq_size = mesh.shape["seq"]
    tp_size = mesh.shape["tp"]
    split = (seq_size // 16, 4, 2, 2, tp_size)
    fine_mesh = Mesh(mesh.devices.reshape(split), ("z", "yh", "yl", "c", "tp"))
    seq_spec = SEQ
    in_specs = (
        P(seq_spec, None),
        P(None, "tp"),
        P(None, "tp"),
        P(None, "tp"),
        P("tp", None),
        P(seq_spec, "tp"),
        P(seq_spec, "tp"),
        P(seq_spec, None),
        P(SEQ + ("tp",), None),
        P(SEQ + ("tp",), None),
        P(seq_spec, None, None),
        P(seq_spec, None, None),
    )
    out_specs = (P(SEQ + ("tp",), None),) * 3
    return jax.shard_map(
        body, mesh=fine_mesh, in_specs=in_specs, out_specs=out_specs, check_vma=False
    )
```

profile of v0, /device:TPU:84, one launch (start us, length us, event | category | flops | bytes accessed | tf_op | source)
XLA Modules:
  0.0 280.1 jit_solution(2323323206248349324)
XLA Ops:
  8.0 0.0 all-gather.4.cloned.1.call-start
  8.1 1.4 pad_maximum_fusion.3
  9.5 0.0 all-gather.4.cloned.1.call-update
  9.5 0.0 reduce-scatter.2.cloned.1.call-start
  9.6 0.8 fusion.25
  10.4 1.2 fusion.15
  11.6 0.8 compare_and_fusion
  12.4 0.1 multiply_cosine_fusion
  12.6 1.5 fusion.37
  14.0 2.0 fusion.35
  16.1 0.3 fusion.41
  16.4 0.1 fusion.20
  16.5 0.3 convolution_convert_fusion.1
  16.8 81.4 %all-gather.4.cloned.1.call-done = bf16[4096,256]{1,0:T(8,128)(2,1)} async-done(((bf16[32,256]{1,0:T(8,128)(2,1)}), bf16[4096,256]{1,0:T(8,128)(2,1)}) %all-gather.4.cloned.1.call-update) | async-done | bytes 2097168 | tf_op jit(solution)/shard_map/all_gather | solution.py:97
  98.2 3.0 %fusion.40 = (bf16[4096,128]{1,0:T(8,128)(2,1)}, bf16[4096,128]{1,0:T(8,128)(2,1)}) fusion(bf16[4096,256]{1,0:T(8,128)(2,1)} %all-gather.4.cloned.1.call-done), kind=kLoop, calls=%fused_computation.72 | loop fusion | bytes 4194304 | tf_op jit(solution)/shard_map/slice | solution.py:99
  101.2 1.5 copy.53
  102.7 2.3 copy.52
  105.0 3.1 %bitcast_reduce_fusion = (f32[128,2,3]{0,2,1:T(4,128)S(1)}, f32[2,4096,128,3]{2,1,3,0:T(8,128)S(1)}) fusion(bf16[4096,2,64,1]{0,2,3,1:T(8,128)(2,1)} %bitcast.80, bf16[128,2,3,32]{0,3,2,1:T(8,128)(2,1)S(1)} %bitcast.88, bf16[128,2,3,32]{0,3,2,1:T(8,128)(2,1)S(1)} %bitcast.86), kind=kOutput, calls=%fused_computation.1 | convolution fusion | flops 409140480 | bytes 13732864 | tf_op jit(solution)/shard_map/tkgd,pkd->tkgp/dot_general | solution.py:105
  108.0 2.0 fusion.1
  110.1 2.3 fusion.10
  112.4 0.2 fusion.13
  112.6 1.3 fusion.42
  113.9 0.0 reduce-scatter.2.cloned.1.call-update
  113.9 0.0 all-gather.6.cloned.1.call-start
  114.0 0.5 all-gather.6.cloned.1.call-update
  114.5 0.1 copy.55
  114.6 0.1 convert_reduce_fusion.1
  114.7 0.1 reduce_window_sum.11
  114.8 0.7 select_reduce_fusion.1
  115.4 0.1 copy.56
  115.5 0.1 copy.57
  115.6 0.2 fusion.19
  115.8 22.7 %reduce-scatter.2.cloned.1.call-done = f32[32,1536]{1,0:T(8,128)} async-done(((f32[128,1536]{1,0:T(8,128)}), f32[32,1536]{1,0:T(8,128)}) %reduce-scatter.2.cloned.1.call-update) | async-done | bytes 196624 | tf_op jit(solution)/shard_map/reduce_scatter | solution.py:126
  138.5 1.1 multiply_reduce_fusion
  139.6 2.7 convolution_convert_fusion
  142.3 12.8 %all-to-all-start = ((bf16[32,16,1536]{2,1,0:T(8,128)(2,1)}), bf16[32,16,1536]{2,1,0:T(8,128)(2,1)S(1)}, u32[]{:S(2)}, u32[]{:S(2)}) async-start(bf16[32,16,1536]{2,1,0:T(8,128)(2,1)} %bitcast.21), calls=%async_computation.1 | async-start | bytes 3145728 | tf_op jit(solution)/shard_map/all_to_all | solution.py:153
  155.1 0.2 all-gather.8.cloned.1.call-start
  155.3 0.4 all-gather.8.cloned.1.call-update
  155.7 14.9 %all-gather.6.cloned.1.call-done = bf16[4,1536,256]{2,1,0:T(8,128)(2,1)} async-done(((bf16[1,1536,256]{2,1,0:T(8,128)(2,1)}), bf16[4,1536,256]{2,1,0:T(8,128)(2,1)}) %all-gather.6.cloned.1.call-update) | async-done | bytes 3145744 | tf_op jit(solution)/shard_map/all_gather | solution.py:155
  170.5 26.1 %all-to-all-done = bf16[32,16,1536]{2,1,0:T(8,128)(2,1)S(1)} async-done(((bf16[32,16,1536]{2,1,0:T(8,128)(2,1)}), bf16[32,16,1536]{2,1,0:T(8,128)(2,1)S(1)}, u32[]{:S(2)}, u32[]{:S(2)}) %all-to-all-start) | async-done | bytes 1572896 | tf_op jit(solution)/shard_map/all_to_all | solution.py:153
  196.7 5.1 %convolution_bitcast_fusion = f32[4,512,256]{2,1,0:T(8,128)} fusion(bf16[512,1536,1]{1,0,2:T(8,128)(2,1)S(1)} %bitcast.81, bf16[4,1536,256]{2,1,0:T(8,128)(2,1)} %all-gather.6.cloned.1.call-done), kind=kOutput, calls=%fused_computation.8 | convolution fusion | flops 1610612736 | bytes 6815744 | tf_op jit(solution)/shard_map/rd,pdf->prf/dot_general | solution.py:157
  201.8 3.8 %all-gather.8.cloned.1.call-done = bf16[4,128,1536]{2,1,0:T(8,128)(2,1)} async-done(((bf16[1,128,1536]{2,1,0:T(8,128)(2,1)}), bf16[4,128,1536]{2,1,0:T(8,128)(2,1)}) %all-gather.8.cloned.1.call-update) | async-done | bytes 1572880 | tf_op jit(solution)/shard_map/all_gather | solution.py:156
  205.5 5.4 %convert_reduce_fusion = bf16[512,1536]{1,0:T(8,128)(2,1)} fusion(bf16[4,128,1536]{2,1,0:T(8,128)(2,1)} %all-gather.8.cloned.1.call-done, f32[4,512,256]{2,1,0:T(8,128)} %convolution_bitcast_fusion), kind=kOutput, calls=%fused_computation.5 | convolution fusion | flops 812384256 | bytes 5242880 | tf_op jit(solution)/shard_map/prf,pfd->prd/dot_general | solution.py:159
  210.9 12.0 %all-to-all-start.1 = ((bf16[32,16,1536]{2,1,0:T(8,128)(2,1)}), bf16[32,16,1536]{2,1,0:T(8,128)(2,1)S(1)}, u32[]{:S(2)}, u32[]{:S(2)}) async-start(bf16[32,16,1536]{2,1,0:T(8,128)(2,1)} %bitcast.82), calls=%async_computation.2 | async-start | bytes 3145728 | tf_op jit(solution)/shard_map/all_to_all | solution.py:163
  222.9 0.1 copy.58
  223.0 0.2 select_reduce_fusion
  223.2 47.9 %all-to-all-done.1 = bf16[32,16,1536]{2,1,0:T(8,128)(2,1)S(1)} async-done(((bf16[32,16,1536]{2,1,0:T(8,128)(2,1)}), bf16[32,16,1536]{2,1,0:T(8,128)(2,1)S(1)}, u32[]{:S(2)}, u32[]{:S(2)}) %all-to-all-start.1) | async-done | bytes 1572896 | tf_op jit(solution)/shard_map/all_to_all | solution.py:163
  271.1 1.5 add_convert_fusion
  (22 shorter events, 0.1 us)
Async XLA Ops:
  8.0 104.6 %copy-start = (bf16[384,1536]{1,0:T(8,128)(2,1)S(1)}, bf16[384,1536]{1,0:T(8,128)(2,1)}, u32[]{:S(2)}) copy-start(bf16[384,1536]{1,0:T(8,128)(2,1)} %param.16) | copy-start | bytes 3538948
  8.0 90.2 %all-gather.4.cloned.1.call-start = ((), (), s32[]{:S(2)}) async-start(), calls=%async_computation.3 | async-start | bytes 2113536 | tf_op jit(solution)/shard_map/all_gather | solution.py:97
  9.5 129.0 %reduce-scatter.2.cloned.1.call-start = ((), (), s32[]{:S(2)}) async-start(), calls=%async_computation.4 | async-start | bytes 983040 | tf_op jit(solution)/shard_map/reduce_scatter | solution.py:126
  11.5 4.9 %copy-start.1 = (bf16[128,1536]{1,0:T(8,128)(2,1)S(1)}, bf16[128,1536]{1,0:T(8,128)(2,1)}, u32[]{:S(2)}) copy-start(bf16[128,1536]{1,0:T(8,128)(2,1)} %param.12) | copy-start | bytes 1179652
  11.5 4.9 %copy-start.3 = (bf16[1536,128]{1,0:T(8,128)(2,1)S(1)}, bf16[1536,128]{1,0:T(8,128)(2,1)}, u32[]{:S(2)}) copy-start(bf16[1536,128]{1,0:T(8,128)(2,1)} %param.15) | copy-start | bytes 1179652
  112.4 2.1 copy-start.4
  113.9 56.6 %all-gather.6.cloned.1.call-start = ((), (), s32[]{:S(2)}) async-start(), calls=%async_computation.5 | async-start | bytes 3932160 | tf_op jit(solution)/shard_map/all_gather | solution.py:155
  142.3 54.4 %all-to-all-start = ((bf16[32,16,1536]{2,1,0:T(8,128)(2,1)}), bf16[32,16,1536]{2,1,0:T(8,128)(2,1)S(1)}, u32[]{:S(2)}, u32[]{:S(2)}) async-start(bf16[32,16,1536]{2,1,0:T(8,128)(2,1)} %bitcast.21), calls=%async_computation.1 | async-start | bytes 3145728 | tf_op jit(solution)/shard_map/all_to_all | solution.py:153
  155.1 50.4 %all-gather.8.cloned.1.call-start = ((), (), s32[]{:S(2)}) async-start(), calls=%async_computation.6 | async-start | bytes 1966080 | tf_op jit(solution)/shard_map/all_gather | solution.py:156
  210.9 12.0 %copy-start.5 = (f32[32,8]{0,1:T(8,128)S(1)}, f32[32,8]{0,1:T(8,128)}, u32[]{:S(2)}) copy-start(f32[32,8]{0,1:T(8,128)} %param.21) | copy-start | bytes 3076
  210.9 60.3 %copy-start.2 = (f32[32,1536]{1,0:T(8,128)S(1)}, f32[32,1536]{1,0:T(8,128)}, u32[]{:S(2)}) copy-start(f32[32,1536]{1,0:T(8,128)} %reduce-scatter.2.cloned.1.call-done) | copy-start | bytes 589828
  210.9 60.3 %all-to-all-start.1 = ((bf16[32,16,1536]{2,1,0:T(8,128)(2,1)}), bf16[32,16,1536]{2,1,0:T(8,128)(2,1)S(1)}, u32[]{:S(2)}, u32[]{:S(2)}) async-start(bf16[32,16,1536]{2,1,0:T(8,128)(2,1)} %bitcast.82), calls=%async_computation.2 | async-start | bytes 3145728 | tf_op jit(solution)/shard_map/all_to_all | solution.py:163
Sparse Core Ops, SparseCore 0:
  12.5 85.6 all-gather.3
  114.0 24.4 reduce-scatter.1
Sparse Core Ops, SparseCore 1:
  116.5 54.0 all-gather.5
  172.5 32.9 all-gather.7
where the time goes:
time: 281 us; the launch traced here: 280 us
  waiting for transfers between devices  198 us (70%)
  matrix products  25.6 us (9%)
  starting transfers between devices  25.1 us (9%)
  between operations  15.7 us (6%)
  other arithmetic  8.96 us (3%)
  local copies, waits for them, and re-layouts  7.04 us (3%)
    all_gather x1, waiting for transfers between devices, body(): whole_both = lax.all_gather(prefix_both, SEQ, axis=0, tiled=True)  81.4 us
    all_to_all x1, waiting for transfers between devices, body(): lax.all_to_all(part_total.reshape(experts, capacity, column_list), EXPERT...  47.9 us
    all_to_all x1, waiting for transfers between devices, body(): lax.all_to_all(outgoing, EXPERT_AXES, split_axis=0, concat_axis=0, tiled=...  26.1 us
    reduce_scatter x1, waiting for transfers between devices, body(): lax.psum_scatter(jnp.dot(attended, w_out, preferred_element_type=jnp.floa...  22.7 us
    all_gather x1, waiting for transfers between devices, body(): full_in = lax.all_gather(expert_in, PART_AXES, axis=0, tiled=True)  14.9 us
    all_to_all x1, starting transfers between devices, body(): lax.all_to_all(outgoing, EXPERT_AXES, split_axis=0, concat_axis=0, tiled=...  12.8 us
    all_to_all x1, starting transfers between devices, body(): lax.all_to_all(part_total.reshape(experts, capacity, column_list), EXPERT...  12 us
  transfers between devices with their start and end apart: 6, of which 6 were waited for; matrix products, arithmetic and copies ran while one was open for 6% of the time, Pallas kernels for 0%

commit v1 on v0

--- a/solution.py
+++ b/solution.py
@@ -152,7 +152,9 @@
     outgoing = gathered.reshape(experts, capacity, column_list)
     incoming = lax.all_to_all(outgoing, EXPERT_AXES, split_axis=0, concat_axis=0, tiled=True)
     incoming = incoming.reshape(experts * capacity, column_list)
-    full_in = lax.all_gather(expert_in, PART_AXES, axis=0, tiled=True)
+    full_in = jnp.concatenate(
+        lax.all_to_all(jnp.stack([expert_in] * lax.axis_size(PART_AXES)), PART_AXES, 0, 0), axis=0
+    )
     full_out = lax.all_gather(expert_out, PART_AXES, axis=0, tiled=True)
     gate_up = jnp.einsum("rd,pdf->prf", incoming, full_in, preferred_element_type=jnp.float32)
     activated = (jax.nn.silu(gate_up[..., :ff_part]) * gate_up[..., ff_part:]).astype(jnp.bfloat16)

time: 281 us -> 275 us (0.979)
  the two profiles are of different devices: /device:TPU:84 before, /device:TPU:24 now
where the time goes in v1:
time: 275 us
  waiting for transfers between devices  190 us (69%)
  starting transfers between devices  29.3 us (11%)
  matrix products  23.1 us (8%)
  between operations  15.7 us (6%)
  local copies, waits for them, and re-layouts  10.2 us (4%)
  other arithmetic  6.49 us (2%)
    all_gather x1, waiting for transfers between devices, body(): whole_both = lax.all_gather(prefix_both, SEQ, axis=0, tiled=True)  79.5 us
    all_to_all x1, waiting for transfers between devices, body(): lax.all_to_all(part_total.reshape(experts, capacity, column_list), EXPERT...  43.1 us
    all_to_all x1, waiting for transfers between devices, body(): lax.all_to_all(outgoing, EXPERT_AXES, split_axis=0, concat_axis=0, tiled=...  43 us
    reduce_scatter x1, waiting for transfers between devices, body(): lax.psum_scatter(jnp.dot(attended, w_out, preferred_element_type=jnp.floa...  24 us
    all_to_all x1, starting transfers between devices, body(): lax.all_to_all(outgoing, EXPERT_AXES, split_axis=0, concat_axis=0, tiled=...  12.1 us
    all_to_all x1, starting transfers between devices, body(): lax.all_to_all(part_total.reshape(experts, capacity, column_list), EXPERT...  11.8 us
  transfers between devices with their start and end apart: 6, of which 4 were waited for; matrix products, arithmetic and copies ran while one was open for 11% of the time, Pallas kernels for 0%

profile of v1, /device:TPU:24, one launch (start us, length us, event | category | flops | bytes accessed | tf_op | source)
XLA Modules:
  0.0 274.8 jit_solution(11552152033732922873)
XLA Ops:
  8.0 0.0 copy-start
  8.0 0.0 all-gather.3.cloned.1.call-start
  8.1 1.4 pad_maximum_fusion.3
  9.5 0.0 all-gather.3.cloned.1.call-update
  9.5 3.0 %stack.2 = bf16[4,1,1536,256]{3,2,1,0:T(8,128)(2,1)} broadcast(bf16[1536,256]{1,0:T(8,128)(2,1)} %bitcast.89), dimensions={2,3} | broadcast | bytes 3932160 | tf_op jit(solution)/shard_map/stack | solution.py:156
  12.5 5.2 %all-to-all-start.1 = ((bf16[4,1,1536,256]{3,2,1,0:T(8,128)(2,1)}), bf16[4,1,1536,256]{3,2,1,0:T(8,128)(2,1)}, u32[]{:S(2)}, u32[]{:S(2)}) async-start(bf16[4,1,1536,256]{3,2,1,0:T(8,128)(2,1)} %stack.2), calls=%async_computation.2 | async-start | bytes 6291456 | tf_op jit(solution)/shard_map/all_to_all | solution.py:156
  17.8 0.1 fusion.30
  17.9 0.2 fusion.20
  18.1 0.1 compare_and_fusion
  18.1 0.1 multiply_cosine_fusion
  18.3 0.4 fusion.42
  18.7 0.6 fusion.40
  19.3 0.3 fusion.46
  19.6 0.1 fusion.25
  19.7 0.3 convolution_convert_fusion.1
  20.1 79.5 %all-gather.3.cloned.1.call-done = bf16[4096,256]{1,0:T(8,128)(2,1)} async-done(((bf16[32,256]{1,0:T(8,128)(2,1)}), bf16[4096,256]{1,0:T(8,128)(2,1)}) %all-gather.3.cloned.1.call-update) | async-done | bytes 2097168 | tf_op jit(solution)/shard_map/all_gather | solution.py:97
  99.6 3.1 %fusion.45 = (bf16[4096,128]{1,0:T(8,128)(2,1)}, bf16[4096,128]{1,0:T(8,128)(2,1)}) fusion(bf16[4096,256]{1,0:T(8,128)(2,1)} %all-gather.3.cloned.1.call-done), kind=kLoop, calls=%fused_computation.74 | loop fusion | bytes 4194304 | tf_op jit(solution)/shard_map/slice | solution.py:99
  102.6 1.5 copy.53
  104.1 2.3 copy.52
  106.4 3.1 %bitcast_reduce_fusion = (f32[128,2,3]{0,2,1:T(4,128)S(1)}, f32[2,4096,128,3]{2,1,3,0:T(8,128)S(1)}) fusion(bf16[4096,2,64,1]{0,2,3,1:T(8,128)(2,1)} %bitcast.85, bf16[128,2,3,32]{0,3,2,1:T(8,128)(2,1)S(1)} %bitcast.94, bf16[128,2,3,32]{0,3,2,1:T(8,128)(2,1)S(1)} %bitcast.92), kind=kOutput, calls=%fused_computation.1 | convolution fusion | flops 409140480 | bytes 13732864 | tf_op jit(solution)/shard_map/tkgd,pkd->tkgp/dot_general | solution.py:105
  109.5 2.0 fusion.1
  111.6 2.3 fusion.15
  113.8 0.0 copy-start.6
  113.8 0.2 fusion.18
  114.1 1.3 fusion.47
  115.3 0.0 reduce-scatter.2.cloned.1.call-update
  115.4 0.1 copy.55
  115.5 0.1 convert_reduce_fusion.1
  115.6 0.1 reduce_window_sum.11
  115.6 0.7 select_reduce_fusion.1
  116.3 0.1 copy.56
  116.4 0.1 copy.57
  116.5 0.2 fusion.24
  116.7 24.0 %reduce-scatter.2.cloned.1.call-done = f32[32,1536]{1,0:T(8,128)} async-done(((f32[128,1536]{1,0:T(8,128)}), f32[32,1536]{1,0:T(8,128)}) %reduce-scatter.2.cloned.1.call-update) | async-done | bytes 196624 | tf_op jit(solution)/shard_map/reduce_scatter | solution.py:126
  140.7 1.1 multiply_reduce_fusion
  141.8 2.7 convolution_convert_fusion
  144.5 0.0 all-to-all-done.1
  144.5 12.1 %all-to-all-start = ((bf16[32,16,1536]{2,1,0:T(8,128)(2,1)}), bf16[32,16,1536]{2,1,0:T(8,128)(2,1)S(1)}, u32[]{:S(2)}, u32[]{:S(2)}) async-start(bf16[32,16,1536]{2,1,0:T(8,128)(2,1)} %bitcast.21), calls=%async_computation.1 | async-start | bytes 3145728 | tf_op jit(solution)/shard_map/all_to_all | solution.py:153
  156.6 0.2 all-gather.5.cloned.1.call-start
  156.9 0.3 all-gather.5.cloned.1.call-update
  157.2 43.0 %all-to-all-done = bf16[32,16,1536]{2,1,0:T(8,128)(2,1)S(1)} async-done(((bf16[32,16,1536]{2,1,0:T(8,128)(2,1)}), bf16[32,16,1536]{2,1,0:T(8,128)(2,1)S(1)}, u32[]{:S(2)}, u32[]{:S(2)}) %all-to-all-start) | async-done | bytes 1572896 | tf_op jit(solution)/shard_map/all_to_all | solution.py:153
  200.2 5.0 %fusion.7 = f32[4,512,256]{2,1,0:T(8,128)} fusion(bf16[512,1536,1]{1,0,2:T(8,128)(2,1)S(1)} %bitcast.86, bf16[4,1,1536,256]{3,2,1,0:T(8,128)(2,1)} %all-to-all-done.1), kind=kOutput, calls=%fused_computation.10 | convolution fusion | flops 1610612736 | bytes 6815744 | tf_op jit(solution)/shard_map/rd,pdf->prf/dot_general | solution.py:159
  205.3 5.4 %convert_reduce_fusion = bf16[512,1536]{1,0:T(8,128)(2,1)} fusion(bf16[4,128,1536]{2,1,0:T(8,128)(2,1)} %all-gather.5.cloned.1.call-done, f32[4,512,256]{2,1,0:T(8,128)} %fusion.7), kind=kOutput, calls=%fused_computation.5 | convolution fusion | flops 812384256 | bytes 5242880 | tf_op jit(solution)/shard_map/prf,pfd->prd/dot_general | solution.py:161
  210.7 11.8 %all-to-all-start.2 = ((bf16[32,16,1536]{2,1,0:T(8,128)(2,1)}), bf16[32,16,1536]{2,1,0:T(8,128)(2,1)S(1)}, u32[]{:S(2)}, u32[]{:S(2)}) async-start(bf16[32,16,1536]{2,1,0:T(8,128)(2,1)} %bitcast.87), calls=%async_computation.3 | async-start | bytes 3145728 | tf_op jit(solution)/shard_map/all_to_all | solution.py:165
  222.4 0.1 copy.58
  222.5 0.2 select_reduce_fusion
  222.7 43.1 %all-to-all-done.2 = bf16[32,16,1536]{2,1,0:T(8,128)(2,1)S(1)} async-done(((bf16[32,16,1536]{2,1,0:T(8,128)(2,1)}), bf16[32,16,1536]{2,1,0:T(8,128)(2,1)S(1)}, u32[]{:S(2)}, u32[]{:S(2)}) %all-to-all-start.2) | async-done | bytes 1572896 | tf_op jit(solution)/shard_map/all_to_all | solution.py:165
  265.9 1.5 add_convert_fusion
  (28 shorter events, 0.1 us)
Async XLA Ops:
  8.0 106.1 %copy-start = (bf16[384,1536]{1,0:T(8,128)(2,1)S(1)}, bf16[384,1536]{1,0:T(8,128)(2,1)}, u32[]{:S(2)}) copy-start(bf16[384,1536]{1,0:T(8,128)(2,1)} %param.16) | copy-start | bytes 3538948
  8.0 91.6 %all-gather.3.cloned.1.call-start = ((), (), s32[]{:S(2)}) async-start(), calls=%async_computation.4 | async-start | bytes 2113536 | tf_op jit(solution)/shard_map/all_gather | solution.py:97
  12.5 5.2 %copy-start.8 = (s32[1,128]{1,0:T(1,128)S(1)}, s32[1,128]{1,0:T(1,128)}, u32[]{:S(2)}) copy-start(s32[1,128]{1,0:T(1,128)} %param.19) | copy-start | bytes 1540
  12.5 5.3 %copy-start.1 = (bf16[128,1536]{1,0:T(8,128)(2,1)S(1)}, bf16[128,1536]{1,0:T(8,128)(2,1)}, u32[]{:S(2)}) copy-start(bf16[128,1536]{1,0:T(8,128)(2,1)} %param.12) | copy-start | bytes 1179652
  12.5 5.8 %copy-start.4 = (bf16[1536,128]{1,0:T(8,128)(2,1)S(1)}, bf16[1536,128]{1,0:T(8,128)(2,1)}, u32[]{:S(2)}) copy-start(bf16[1536,128]{1,0:T(8,128)(2,1)} %param.14) | copy-start | bytes 1179652
  12.5 6.1 %copy-start.3 = (bf16[1536,384]{1,0:T(8,128)(2,1)S(1)}, bf16[1536,384]{1,0:T(8,128)(2,1)}, u32[]{:S(2)}) copy-start(bf16[1536,384]{1,0:T(8,128)(2,1)} %param.13) | copy-start | bytes 3538948
  12.5 132.0 %all-to-all-start.1 = ((bf16[4,1,1536,256]{3,2,1,0:T(8,128)(2,1)}), bf16[4,1,1536,256]{3,2,1,0:T(8,128)(2,1)}, u32[]{:S(2)}, u32[]{:S(2)}) async-start(bf16[4,1,1536,256]{3,2,1,0:T(8,128)(2,1)} %stack.2), calls=%async_computation.2 | async-start | bytes 6291456 | tf_op jit(solution)/shard_map/all_to_all | solution.py:156
  17.7 123.0 %reduce-scatter.2.cloned.1.call-start = ((), (), s32[]{:S(2)}) async-start(), calls=%async_computation.5 | async-start | bytes 983040 | tf_op jit(solution)/shard_map/reduce_scatter | solution.py:126
  18.0 1.7 copy-start.5
  113.8 1.5 copy-start.6
  144.5 55.7 %all-to-all-start = ((bf16[32,16,1536]{2,1,0:T(8,128)(2,1)}), bf16[32,16,1536]{2,1,0:T(8,128)(2,1)S(1)}, u32[]{:S(2)}, u32[]{:S(2)}) async-start(bf16[32,16,1536]{2,1,0:T(8,128)(2,1)} %bitcast.21), calls=%async_computation.1 | async-start | bytes 3145728 | tf_op jit(solution)/shard_map/all_to_all | solution.py:153
  156.6 48.7 %all-gather.5.cloned.1.call-start = ((), (), s32[]{:S(2)}) async-start(), calls=%async_computation.6 | async-start | bytes 1966080 | tf_op jit(solution)/shard_map/all_gather | solution.py:158
  210.7 11.8 %copy-start.7 = (f32[32,8]{0,1:T(8,128)S(1)}, f32[32,8]{0,1:T(8,128)}, u32[]{:S(2)}) copy-start(f32[32,8]{0,1:T(8,128)} %param.21) | copy-start | bytes 3076
  210.7 55.2 %copy-start.2 = (f32[32,1536]{1,0:T(8,128)S(1)}, f32[32,1536]{1,0:T(8,128)}, u32[]{:S(2)}) copy-start(f32[32,1536]{1,0:T(8,128)} %reduce-scatter.2.cloned.1.call-done) | copy-start | bytes 589828
  210.7 55.2 %all-to-all-start.2 = ((bf16[32,16,1536]{2,1,0:T(8,128)(2,1)}), bf16[32,16,1536]{2,1,0:T(8,128)(2,1)S(1)}, u32[]{:S(2)}, u32[]{:S(2)}) async-start(bf16[32,16,1536]{2,1,0:T(8,128)(2,1)} %bitcast.87), calls=%async_computation.3 | async-start | bytes 3145728 | tf_op jit(solution)/shard_map/all_to_all | solution.py:165
Sparse Core Ops, SparseCore 0:
  12.5 87.0 all-gather.2
  115.5 25.1 reduce-scatter.1
Sparse Core Ops, SparseCore 1:
  159.2 42.3 all-gather.4
